TPU v7x, 256 devices: a whole 4x4x8 slice. The times are simulated.
256 devices in a mesh: pair: 2 (over core), seq: 32 (over y, x, z_hi), tp: 4 (over z_lo).
Axes of the slice: x: 4, y: 4, z: 8 (z_hi: 2, z_lo: 4; z = z_hi * 4 + z_lo), core: 2. Of those that a mesh axis runs over, the one named last changes fastest.
Arguments:
- hidden: bfloat16 [36864, 3072], P(('pair', 'seq'), 'tp'), may hold values from -11 to 11
- positions: int32 [3, 36864], P(None, ('pair', 'seq')), may hold values from 0 to 63, as said below
- lengths: int32 [8], P('pair'), may hold values from 1 to 512, as said below
- step_index: int32 [1], replicated, may hold values from 0 to 7
- layer_mod: float32 [8, 3, 3072], P('pair'), may hold values from -3 to 3
- final_mod: float32 [8, 2, 3072], P('pair'), may hold values from -3 to 3
- qkv_weight: bfloat16 [3072, 3, 1536], P(None, None, 'tp'), may hold values from -0.108253175 to 0.108253175
- q_gain: float32 [128], replicated, may hold values from 0.5 to 5.5
- k_gain: float32 [128], replicated, may hold values from 0.5 to 5.5
- out_weight: bfloat16 [1536, 3072], P('tp'), may hold values from -0.15625 to 0.15625
- final_weight: bfloat16 [3072, 64], P('tp'), may hold values from -0.109375 to 0.109375
- latents: float32 [16384, 64], P(('pair', 'seq')), may hold values from -6 to 6
Outputs:
- new_hidden: bfloat16 [36864, 3072], P(('pair', 'seq'), 'tp')
- attention_lse: float32 [12, 36864], P('tp', ('pair', 'seq'))
- next_latents: float32 [16384, 64], P(('pair', 'seq'))
Inputs may be any that keep to these rules, and one draw needn't show every extreme that they name: `lengths`: some sequence has all 512 text tokens live and some sequence just one. `positions`: the first component is zero; text rows are zero; the image rows of a sequence hold each cell (row, column) of a grid 64 cells wide exactly once, the same for both sequences of a prompt.
All inputs are finite; a program needn't handle non-finite values.
Results may differ from a plain program's by a relative error of at most 0.01.
Values may be sent and summed in bfloat16 or wider, within the bound.
No kernel may reach another device: no remote copies, remote signals or barrier semaphores. Data moves between devices by JAX's collectives and lax.ppermute only.
A program may use at most 128 MiB of HBM per device.

v0:
```python
import jax
import jax.numpy as jnp
from jax import lax
from jax.sharding import PartitionSpec as P

ROPE_T = 16
ROPE_H = 56
ROPE_W = 56
STEPS = 8
IMG_DEV = 512
TXT_DEV = 64
GUIDE = 3.5
SHIFT = 3.0


def swapped(block, axis, bit):
    count = lax.axis_size(axis)
    route = []
    for low in range(count):
        high = low | 1 << bit
        if high != low and high < count:
            route += [(low, high), (high, low)]
    return lax.ppermute(block, axis, route)


def rope_angles(ids_block):
    angle_parts = []
    for axis_pos, rope_width in ((0, ROPE_T), (1, ROPE_H), (2, ROPE_W)):
        frequencies = 10000.0 ** (-jnp.arange(0, rope_width, 2).astype(jnp.float32) / rope_width)
        angle_parts.append(ids_block[axis_pos].astype(jnp.float32)[:, None] * frequencies[None, :])
    angles = jnp.concatenate(angle_parts, axis=1)
    return (jnp.cos(angles), jnp.sin(angles))


def rotate(tensor, cosine, sine_part):
    dims_in = tensor.shape
    pair_view = tensor.reshape(dims_in[0], dims_in[1], dims_in[2] // 2, 2)
    first_part = pair_view[..., 0]
    second_part = pair_view[..., 1]
    cosine = cosine[:, None, :]
    sine_part = sine_part[:, None, :]
    turned = jnp.stack(
        [
            cosine * first_part - sine_part * second_part,
            sine_part * first_part + cosine * second_part,
        ],
        axis=-1,
    )
    return turned.reshape(dims_in)


def rms_gain(tensor, gain_vec):
    return tensor * lax.rsqrt(jnp.mean(tensor * tensor, axis=-1, keepdims=True) + 1e-06) * gain_vec


def modulate(features, shift_vec, scale_vec):
    row_mean = jnp.mean(features, axis=-1, keepdims=True)
    row_var = jnp.mean(features * features, axis=-1, keepdims=True) - row_mean * row_mean
    return (features - row_mean) * lax.rsqrt(row_var + 1e-06) * (1.0 + scale_vec) + shift_vec


def sigma_at(step_now):
    time_now = 1.0 - step_now.astype(jnp.float32) / STEPS
    return SHIFT * time_now / (1.0 + (SHIFT - 1.0) * time_now)


def attend_block(softmax_state, queries, packet, anchor, text_count):
    rows_dev = IMG_DEV + TXT_DEV
    piece_count = packet.shape[1] // rows_dev
    offset = jnp.arange(rows_dev, dtype=jnp.int32)
    score_scale = queries.shape[-1] ** (-0.5)

    def fold_piece(piece_idx, carried):
        row_max, row_sum, weighted = carried
        key_piece = lax.dynamic_slice_in_dim(packet, piece_idx * rows_dev, rows_dev, 1)
        text_index = (anchor + piece_idx) * TXT_DEV + offset - IMG_DEV
        is_live = (offset < IMG_DEV) | (text_index < text_count)
        scores = (
            jnp.einsum("qhd,khd->hqk", queries, key_piece[0], preferred_element_type=jnp.float32)
            * score_scale
        )
        scores = jnp.where(is_live[None, None, :], scores, -jnp.inf)
        new_max = jnp.maximum(row_max, jnp.max(scores, axis=2))
        exps = jnp.exp(scores - new_max[:, :, None])
        decay = jnp.exp(row_max - new_max)
        row_sum = row_sum * decay + jnp.sum(exps, axis=2)
        weighted = weighted * decay[:, :, None] + jnp.einsum(
            "hqk,khd->hqd",
            exps.astype(jnp.bfloat16),
            key_piece[1],
            preferred_element_type=jnp.float32,
        )
        return (new_max, row_sum, weighted)

    return lax.fori_loop(0, piece_count, fold_piece, softmax_state)


def on_device(
    hidden,
    positions,
    lengths,
    step_index,
    layer_mod,
    final_mod,
    qkv_weight,
    q_gain,
    k_gain,
    out_weight,
    final_weight,
    latents,
):
    spread = lax.axis_size("seq") // 4
    bit_count = spread.bit_length() - 1
    seq_pos = lax.axis_index("seq")
    local_seq = seq_pos // spread
    shard_pos = seq_pos % spread
    tp_pos = lax.axis_index("tp")
    local_width = hidden.shape[1]
    gathered = lax.all_gather(hidden, "tp", axis=1, tiled=True)
    model_width = gathered.shape[1]
    rows_dev = gathered.shape[0]
    layer_terms = lax.dynamic_index_in_dim(layer_mod, local_seq, 0, keepdims=False)
    text_count = lax.dynamic_index_in_dim(lengths, local_seq, 0, keepdims=False)
    modulated = modulate(gathered.astype(jnp.float32), layer_terms[0], layer_terms[1]).astype(
        jnp.bfloat16
    )
    head_dim = q_gain.shape[0]
    head_cols = qkv_weight.shape[2]
    heads_here = head_cols // head_dim
    projected = jnp.dot(
        modulated,
        qkv_weight.reshape(model_width, 3 * head_cols),
        preferred_element_type=jnp.float32,
    )
    projected = projected.reshape(rows_dev, 3, heads_here, head_dim)
    cosine, sine_part = rope_angles(positions)
    queries = rotate(rms_gain(projected[:, 0], q_gain), cosine, sine_part).astype(jnp.bfloat16)
    key_rot = rotate(rms_gain(projected[:, 1], k_gain), cosine, sine_part).astype(jnp.bfloat16)
    values = projected[:, 2].astype(jnp.bfloat16)
    packet = jnp.stack([key_rot, values])
    softmax_state = (
        jnp.full((heads_here, rows_dev), -jnp.inf, jnp.float32),
        jnp.zeros((heads_here, rows_dev), jnp.float32),
        jnp.zeros((heads_here, rows_dev, head_dim), jnp.float32),
    )
    held_keys = packet
    for bit_pos in range(bit_count):
        far_keys = swapped(held_keys, "seq", bit_pos)
        block_size = 1 << bit_pos
        lower_half = shard_pos // block_size % 2 == 0
        held_keys = jnp.where(
            lower_half,
            jnp.concatenate([held_keys, far_keys], axis=1),
            jnp.concatenate([far_keys, held_keys], axis=1),
        )
    softmax_state = attend_block(softmax_state, queries, held_keys, 0, text_count)
    row_max, row_sum, weighted = softmax_state
    attended = (weighted / row_sum[:, :, None]).astype(jnp.bfloat16)
    log_sums = row_max + jnp.log(row_sum)
    attn_flat = attended.transpose(1, 0, 2).reshape(rows_dev, head_cols)
    partial_out = jnp.dot(attn_flat, out_weight, preferred_element_type=jnp.float32)
    update = lax.psum_scatter(
        partial_out.astype(jnp.bfloat16), "tp", scatter_dimension=1, tiled=True
    ).astype(jnp.float32)
    gate_slice = lax.dynamic_slice_in_dim(layer_terms[2], tp_pos * local_width, local_width, 0)
    new_hidden = (hidden.astype(jnp.float32) + gate_slice * update).astype(jnp.bfloat16)
    final_terms = lax.dynamic_index_in_dim(final_mod, local_seq, 0, keepdims=False)
    final_shift = lax.dynamic_slice_in_dim(final_terms[0], tp_pos * local_width, local_width, 0)
    final_scale = lax.dynamic_slice_in_dim(final_terms[1], tp_pos * local_width, local_width, 0)
    image_rows = new_hidden[:IMG_DEV].astype(jnp.float32)
    weight = final_weight.astype(jnp.float32)
    row_sums = jnp.sum(image_rows, axis=1)
    squares = jnp.sum(image_rows * image_rows, axis=1)
    row_sums, squares = lax.psum((row_sums, squares), "tp")
    row_mean = row_sums / model_width
    inv_std = lax.rsqrt(squares / model_width - row_mean * row_mean + 1e-06)
    final_in = (image_rows - row_mean[:, None]) * inv_std[:, None] * (
        1.0 + final_scale
    ) + final_shift
    velocity = lax.psum(
        jnp.dot(final_in, weight, precision=lax.Precision.HIGHEST).astype(jnp.bfloat16), "tp"
    ).astype(jnp.float32)
    half_rows = IMG_DEV // 2
    is_cond = local_seq % 2 == 0
    outgoing = jnp.where(is_cond, velocity[half_rows:], velocity[:half_rows])
    partner_half = swapped(outgoing.astype(jnp.bfloat16), "seq", bit_count).astype(outgoing.dtype)
    own_half = jnp.where(is_cond, velocity[:half_rows], velocity[half_rows:])
    cond_vel = jnp.where(is_cond, own_half, partner_half)
    uncond_vel = jnp.where(is_cond, partner_half, own_half)
    guided = uncond_vel + GUIDE * (cond_vel - uncond_vel)
    step_now = step_index[0]
    time_step = sigma_at(step_now + 1) - sigma_at(step_now)
    return (new_hidden, log_sums, latents + time_step * guided)


def solution(mesh):
    return jax.shard_map(
        on_device,
        mesh=mesh,
        in_specs=(
            P(("pair", "seq"), "tp"),
            P(None, ("pair", "seq")),
            P("pair"),
            P(),
            P("pair", None, None),
            P("pair", None, None),
            P(None, None, "tp"),
            P(),
            P(),
            P("tp", None),
            P("tp", None),
            P(("pair", "seq"), None),
        ),
        out_specs=(P(("pair", "seq"), "tp"), P("tp", ("pair", "seq")), P(("pair", "seq"), None)),
        check_vma=False,
    )
```

profile of v0, /device:TPU:2, one launch (start us, length us, event | category | flops | bytes accessed | tf_op | source)
XLA Modules:
  0.0 560.9 jit_solution(13021237416934958148)
XLA Ops:
  8.0 10.3 %copy.17 = bf16[3072,3,384]{0,2,1:T(8,128)(2,1)} copy(bf16[3072,3,384]{2,0,1:T(8,128)(2,1)} %param.20) | data formatting | bytes 14155776 | tf_op args[6]
  20.3 65.6 %all-gather.2.cloned.1.call-done = bf16[576,3072]{1,0:T(8,128)(2,1)} async-done(((bf16[576,768]{1,0:T(8,128)(2,1)}), bf16[576,3072]{1,0:T(8,128)(2,1)}) %all-gather.2.cloned.1.call-update) | async-done | bytes 3538960 | tf_op jit(solution)/shard_map/all_gather | solution.py:119
  85.9 3.3 convert_reduce_fusion
  89.2 8.0 %fusion.26 = f32[576,3,3,128]{3,0,2,1:T(8,128)S(1)} fusion(bf16[3,3,128,3072]{3,2,1,0:T(8,128)(2,1)} %bitcast.68, bf16[576,3072]{1,0:T(8,128)(2,1)S(1)} %copy-done.1, f32[3072]{0:T(1024)S(1)} %bitcast.71, f32[3072]{0:T(1024)S(1)} %bitcast.70, f32[576]{0:T(1024)S(1)} %get-tuple-element.306, f32[576]{0:T(1024)S(1)} %get-tuple-element.305), kind=kOutput, calls=%fused_computation.38 | convolution fusion | flops 4087480320 | bytes 13300224 | tf_op jit(solution)/shard_map/dot_general | solution.py:130
  112.7 3.4 subtract_convert_fusion
  122.5 4.5 collective-permute-start
  127.0 30.3 %collective-permute-done = bf16[2,576,3,128]{3,1,2,0:T(8,128)(2,1)} collective-permute-done((bf16[2,576,3,128]{3,1,2,0:T(8,128)(2,1)}, bf16[2,576,3,128]{3,1,2,0:T(8,128)(2,1)}, u32[]{:S(2)}, u32[]{:S(2)}) %collective-permute-start) | collective-permute-done | bytes 884768 | tf_op jit(solution)/shard_map/ppermute | solution.py:23
  161.0 39.1 %collective-permute-done.1 = bf16[2,1152,3,128]{3,1,2,0:T(8,128)(2,1)} collective-permute-done((bf16[2,1152,3,128]{3,1,2,0:T(8,128)(2,1)}, bf16[2,1152,3,128]{3,1,2,0:T(8,128)(2,1)}, u32[]{:S(2)}, u32[]{:S(2)}) %collective-permute-start.1) | collective-permute-done | bytes 1769504 | tf_op jit(solution)/shard_map/ppermute | solution.py:23
  200.1 5.3 maximum_select_fusion.1
  211.6 71.9 %collective-permute-done.2 = bf16[2,2304,3,128]{3,1,2,0:T(8,128)(2,1)} collective-permute-done((bf16[2,2304,3,128]{3,1,2,0:T(8,128)(2,1)}, bf16[2,2304,3,128]{3,1,2,0:T(8,128)(2,1)}, u32[]{:S(2)}, u32[]{:S(2)}) %collective-permute-start.2) | collective-permute-done | bytes 3538976 | tf_op jit(solution)/shard_map/ppermute | solution.py:23
  283.5 9.3 %maximum_select_fusion = bf16[2,4608,3,128]{3,1,2,0:T(8,128)(2,1)} fusion(bf16[2,2304,3,128]{3,1,2,0:T(8,128)(2,1)} %collective-permute-done.2, bf16[2,2304,3,128]{3,1,2,0:T(8,128)(2,1)} %maximum_select_fusion.1, pred[]{:T(512)S(6)} %eq.18), kind=kLoop, calls=%fused_computation.35 | loop fusion | flops 31850496 | bytes 14155777 | tf_op jit(solution)/shard_map/jit(_where)/select_n | solution.py:151
  292.8 102.5 %while.21 = (s32[]{:T(128)}, f32[3,576]{1,0:T(4,128)S(1)}, f32[3,576]{1,0:T(4,128)S(1)}, f32[3,576,128]{2,1,0:T(8,128)}, s32[]{:T(128)}, /*index=5*/bf16[2,4608,...) while((s32[]{:T(128)}, f32[3,576]{1,0:T(4,128)S(1)}, ...), condition=%wide.region_7.8_spmd.clone.clone, body=%wide.region_4.7_spmd.clone.clone.sunk | while | flops 521231616 | bytes 15596003 | solution.py:95
  293.5 3.9 bitcast_reduce_fusion.2
  300.7 4.7 fusion.72
  306.1 3.9 bitcast_reduce_fusion.2
  313.3 5.0 fusion.72
  318.9 3.9 bitcast_reduce_fusion.2
  326.1 5.0 fusion.72
  331.7 3.9 bitcast_reduce_fusion.2
  339.0 5.0 fusion.72
  344.6 3.9 bitcast_reduce_fusion.2
  351.8 5.0 fusion.72
  357.4 3.9 bitcast_reduce_fusion.2
  364.7 5.0 fusion.72
  370.3 3.9 bitcast_reduce_fusion.2
  377.5 5.0 fusion.72
  383.1 3.9 bitcast_reduce_fusion.2
  390.3 5.0 fusion.72
  397.1 3.8 convolution_convert_fusion
  402.7 80.0 %reduce-scatter.2.cloned.1.call-done = bf16[576,768]{1,0:T(8,128)(2,1)} async-done(((bf16[576,3072]{1,0:T(8,128)(2,1)}), bf16[576,768]{1,0:T(8,128)(2,1)}) %reduce-scatter.2.cloned.1.call-update) | async-done | bytes 884752 | tf_op jit(solution)/shard_map/reduce_scatter | solution.py:162
  485.4 10.7 %all-reduce = (f32[512]{0:T(512)S(1)}, f32[512]{0:T(512)S(1)}) all-reduce(f32[512]{0:T(512)S(1)} %get-tuple-element.267, f32[512]{0:T(512)S(1)} %get-tuple-element.266), channel_id=1, replica_groups=mesh['pair'=2,'seq'=32,'tp'=4] {'tp'}, use_global_device_ids=true, to_apply=%region_12.13 | all-reduce | flops 1024 | bytes 8192 | tf_op jit(solution)/shard_map/psum | solution.py:174
  499.9 48.9 %all-reduce.3.cloned.1.call-done = bf16[512,64]{0,1:T(8,128)(2,1)} async-done(((bf16[512,64]{0,1:T(8,128)(2,1)}), bf16[512,64]{0,1:T(8,128)(2,1)}) %all-reduce.3.cloned.1.call-update) | async-done | bytes 65552 | tf_op jit(solution)/shard_map/psum | solution.py:180
  (117 shorter events, 80.6 us)
Async XLA Ops:
  7.2 389.9 %copy-start = (bf16[384,3072]{1,0:T(8,128)(2,1)S(1)}, bf16[384,3072]{1,0:T(8,128)(2,1)}, u32[]{:S(2)}) copy-start(bf16[384,3072]{1,0:T(8,128)(2,1)} %param.23) | copy-start | bytes 7077892
  7.2 78.7 %all-gather.2.cloned.1.call-start = ((), (), s32[]{:S(2)}) async-start(), calls=%async_computation.1 | async-start | bytes 4423680 | tf_op jit(solution)/shard_map/all_gather | solution.py:119
  7.9 474.8 %reduce-scatter.2.cloned.1.call-start = ((), (), s32[]{:S(2)}) async-start(), calls=%async_computation.2 | async-start | bytes 4423680 | tf_op jit(solution)/shard_map/reduce_scatter | solution.py:162
  8.0 10.3 %copy-start.8 = (f32[128]{0:T(128)S(1)}, f32[128]{0:T(128)}, u32[]{:S(2)}) copy-start(f32[128]{0:T(128)} %param.22) | copy-start | bytes 1540
  8.0 10.4 %copy-start.9 = (f32[128]{0:T(128)S(1)}, f32[128]{0:T(128)}, u32[]{:S(2)}) copy-start(f32[128]{0:T(128)} %param.21) | copy-start | bytes 1540
  8.0 10.6 %copy-start.7 = (s32[3,576]{1,0:T(4,128)S(1)}, s32[3,576]{1,0:T(4,128)}, u32[]{:S(2)}) copy-start(s32[3,576]{1,0:T(4,128)} %param.15) | copy-start | bytes 20740
  85.9 3.3 copy-start.1
  122.5 34.9 %collective-permute-start = (bf16[2,576,3,128]{3,1,2,0:T(8,128)(2,1)}, bf16[2,576,3,128]{3,1,2,0:T(8,128)(2,1)}, u32[]{:S(2)}, u32[]{:S(2)}) collective-permute-start(bf16[2,576,3,128]{3,1,2,0:T(8,128)(2,1)} %pad_maximum_fusion), channel_id=1, source_target_pairs={{0,4},{4,0},{8,12},{12,8},{16,20},{20,16},{24,28},{28,24},{32,36},... | collective-permute-start | bytes 2654216 | tf_op jit(solution)/shard_map/ppermute | solution.py:23
  160.4 39.7 %collective-permute-start.1 = (bf16[2,1152,3,128]{3,1,2,0:T(8,128)(2,1)}, bf16[2,1152,3,128]{3,1,2,0:T(8,128)(2,1)}, u32[]{:S(2)}, u32[]{:S(2)}) collective-permute-start(bf16[2,1152,3,128]{3,1,2,0:T(8,128)(2,1)} %maximum_select_fusion.2), channel_id=1, source_target_pairs={{0,8},{8,0},{4,12},{12,4},{16,24},{24,16},{20,28},{28,20},{32,40},... | collective-permute-start | bytes 5308424 | tf_op jit(solution)/shard_map/ppermute | solution.py:23
  161.0 46.4 %copy-start.11 = (s32[4]{0:T(128)S(1)}, s32[4]{0:T(128)}, u32[]{:S(2)}) copy-start(s32[4]{0:T(128)} %param.16) | copy-start | bytes 52
  161.0 47.0 %copy-start.4 = (bf16[576,3,64,1]{0,3,2,1:T(2,128)(2,1)S(1)}, bf16[576,3,64,1]{0,3,2,1:T(2,128)(2,1)}, u32[]{:S(2)}) copy-start(bf16[576,3,64,1]{0,3,2,1:T(2,128)(2,1)} %get-tuple-element.295) | copy-start | bytes 663556
  161.0 47.0 %copy-start.5 = (bf16[576,3,64,1]{0,3,2,1:T(2,128)(2,1)S(1)}, bf16[576,3,64,1]{0,3,2,1:T(2,128)(2,1)}, u32[]{:S(2)}) copy-start(bf16[576,3,64,1]{0,3,2,1:T(2,128)(2,1)} %get-tuple-element.296) | copy-start | bytes 663556
  205.4 78.2 %collective-permute-start.2 = (bf16[2,2304,3,128]{3,1,2,0:T(8,128)(2,1)}, bf16[2,2304,3,128]{3,1,2,0:T(8,128)(2,1)}, u32[]{:S(2)}, u32[]{:S(2)}) collective-permute-start(bf16[2,2304,3,128]{3,1,2,0:T(8,128)(2,1)} %maximum_select_fusion.1), channel_id=1, source_target_pairs={{0,16},{16,0},{4,20},{20,4},{8,24},{24,8},{12,28},{28,12},{32,48},... | collective-permute-start | bytes 10616840 | tf_op jit(solution)/shard_map/ppermute | solution.py:23
  400.8 81.8 %copy-start.2 = (bf16[576,768]{1,0:T(8,128)(2,1)S(1)}, bf16[576,768]{1,0:T(8,128)(2,1)}, u32[]{:S(2)}) copy-start(bf16[576,768]{1,0:T(8,128)(2,1)} %param.14) | copy-start | bytes 2654212
  400.8 95.3 %copy-start.10 = (bf16[768,64]{0,1:T(8,128)(2,1)S(1)}, bf16[768,64]{0,1:T(8,128)(2,1)}, u32[]{:S(2)}) copy-start(bf16[768,64]{0,1:T(8,128)(2,1)} %param.24) | copy-start | bytes 294916
  400.9 152.8 %copy-start.6 = (f32[256,64]{0,1:T(8,128)S(1)}, f32[256,64]{0,1:T(8,128)}, u32[]{:S(2)}) copy-start(f32[256,64]{0,1:T(8,128)} %param.25) | copy-start | bytes 196612
  400.9 147.9 %all-reduce.3.cloned.1.call-start = ((), (), s32[]{:S(2)}) async-start(), calls=%async_computation.3 | async-start | bytes 131072 | tf_op jit(solution)/shard_map/psum | solution.py:180
  484.1 0.9 copy-start.3
  549.7 4.0 collective-permute-start.3
Sparse Core Ops, SparseCore 0:
  9.8 76.0 all-gather.1
  401.0 81.6 reduce-scatter.1
  499.3 49.4 all-reduce.2
where the time goes:
time: 563 us; the launch traced here: 561 us
  waiting for transfers between devices  338 us (60%)
  matrix products  85.7 us (15%)
  other arithmetic  73.4 us (13%)
  local copies, waits for them, and re-layouts  28.9 us (5%)
  between operations  14.7 us (3%)
  blocking collectives  10.7 us (2%)
  starting transfers between devices  8.84 us (2%)
    ppermute x4, waiting for transfers between devices, swapped(): return lax.ppermute(block, axis, route)  143 us
    reduce_scatter x1, waiting for transfers between devices, on_device(): lax.psum_scatter(partial_out.astype(jnp.bfloat16), 'tp', scatter_dimensio...  80 us
    all_gather x1, waiting for transfers between devices, on_device(): gathered = lax.all_gather(hidden, 'tp', axis=1, tiled=True)  65.6 us
    psum x1, waiting for transfers between devices, on_device(): lax.psum(jnp.dot(final_in, weight, precision=lax.Precision.HIGHEST).astyp...  48.9 us
    dot_general x8, matrix products, fold_piece(): jnp.einsum('hqk,khd->hqd', exps.astype(jnp.bfloat16), key_piece[1], prefe...  39.4 us
    dot_general x8, matrix products, fold_piece(): jnp.einsum('qhd,khd->hqk', queries, key_piece[0], preferred_element_type=...  31.6 us
    reduce_sum x8, other arithmetic, fold_piece(): row_sum = row_sum * decay + jnp.sum(exps, axis=2)  25.9 us
    select_n x3, other arithmetic, on_device(): jnp.where(lower_half, jnp.concatenate([held_keys, far_keys], axis=1), jnp...  17.7 us
  transfers between devices with their start and end apart: 7, of which 7 were waited for; matrix products, arithmetic and copies ran while one was open for 3% of the time, Pallas kernels for 0%

commit v1 on v0

--- a/solution.py
+++ b/solution.py
@@ -177,7 +177,10 @@
     final_in = (image_rows - row_mean[:, None]) * inv_std[:, None] * (
         1.0 + final_scale
     ) + final_shift
-    velocity = lax.psum(
+    pieces_all_form = lambda u_in, net_axis: jnp.sum(
+        lax.all_gather(u_in, axis_name=net_axis), axis=0
+    )
+    velocity = pieces_all_form(
         jnp.dot(final_in, weight, precision=lax.Precision.HIGHEST).astype(jnp.bfloat16), "tp"
     ).astype(jnp.float32)
     half_rows = IMG_DEV // 2

time: 563 us -> 526 us (0.934)
  waiting for transfers between devices: 338 us -> 289 us
  blocking collectives: 10.7 us -> 24.6 us
    psum x1 -> x0, waiting for transfers between devices: 48.9 us -> none  [on_device(): lax.psum(jnp.dot(final_in, weight, precision=lax.Precision.HIGHEST).astyp...]
    all_gather x0 -> x1, blocking collectives: none -> 13.9 us  [on_device(): lax.all_gather(u_in, axis_name=net_axis)]
  transfers between devices with their start and end apart: 7 -> 6, of which waited for: 7 -> 6; matrix products, arithmetic and copies ran while one was open for 3% -> 4% of each run, Pallas kernels for 0% -> 0%
where the time goes in v1:
time: 526 us; the launch traced here: 524 us
  waiting for transfers between devices  289 us (55%)
  matrix products  85.1 us (16%)
  other arithmetic  72.9 us (14%)
  local copies, waits for them, and re-layouts  29 us (6%)
  blocking collectives  24.6 us (5%)
  between operations  15.1 us (3%)
  starting transfers between devices  8.8 us (2%)
    ppermute x4, waiting for transfers between devices, swapped(): return lax.ppermute(block, axis, route)  143 us
    reduce_scatter x1, waiting for transfers between devices, on_device(): lax.psum_scatter(partial_out.astype(jnp.bfloat16), 'tp', scatter_dimensio...  79.3 us
    all_gather x1, waiting for transfers between devices, on_device(): gathered = lax.all_gather(hidden, 'tp', axis=1, tiled=True)  65.6 us
    dot_general x8, matrix products, fold_piece(): jnp.einsum('hqk,khd->hqd', exps.astype(jnp.bfloat16), key_piece[1], prefe...  39.4 us
    dot_general x8, matrix products, fold_piece(): jnp.einsum('qhd,khd->hqk', queries, key_piece[0], preferred_element_type=...  31.6 us
    reduce_sum x8, other arithmetic, fold_piece(): row_sum = row_sum * decay + jnp.sum(exps, axis=2)  25.9 us
    select_n x3, other arithmetic, on_device(): jnp.where(lower_half, jnp.concatenate([held_keys, far_keys], axis=1), jnp...  17.7 us
    all_gather x1, blocking collectives, on_device(): lax.all_gather(u_in, axis_name=net_axis)  13.9 us
  transfers between devices with their start and end apart: 6, of which 6 were waited for; matrix products, arithmetic and copies ran while one was open for 4% of the time, Pallas kernels for 0%

profile of v1, /device:TPU:2, one launch (start us, length us, event | category | flops | bytes accessed | tf_op | source)
XLA Modules:
  0.0 524.4 jit_solution(2363377369706950411)
XLA Ops:
  8.0 10.3 %copy.17 = bf16[3072,3,384]{0,2,1:T(8,128)(2,1)} copy(bf16[3072,3,384]{2,0,1:T(8,128)(2,1)} %param.20) | data formatting | bytes 14155776 | tf_op args[6]
  20.3 65.6 %all-gather.3.cloned.1.call-done = bf16[576,3072]{1,0:T(8,128)(2,1)} async-done(((bf16[576,768]{1,0:T(8,128)(2,1)}), bf16[576,3072]{1,0:T(8,128)(2,1)}) %all-gather.3.cloned.1.call-update) | async-done | bytes 3538960 | tf_op jit(solution)/shard_map/all_gather | solution.py:119
  85.9 3.3 convert_reduce_fusion
  89.2 8.0 %fusion.26 = f32[576,3,3,128]{3,0,2,1:T(8,128)S(1)} fusion(bf16[3,3,128,3072]{3,2,1,0:T(8,128)(2,1)} %bitcast.70, bf16[576,3072]{1,0:T(8,128)(2,1)S(1)} %copy-done.1, f32[3072]{0:T(1024)S(1)} %bitcast.73, f32[3072]{0:T(1024)S(1)} %bitcast.72, f32[576]{0:T(1024)S(1)} %get-tuple-element.306, f32[576]{0:T(1024)S(1)} %get-tuple-element.305), kind=kOutput, calls=%fused_computation.38 | convolution fusion | flops 4087480320 | bytes 13300224 | tf_op jit(solution)/shard_map/dot_general | solution.py:130
  112.7 3.4 subtract_convert_fusion
  122.5 4.5 collective-permute-start
  127.0 30.3 %collective-permute-done = bf16[2,576,3,128]{3,1,2,0:T(8,128)(2,1)} collective-permute-done((bf16[2,576,3,128]{3,1,2,0:T(8,128)(2,1)}, bf16[2,576,3,128]{3,1,2,0:T(8,128)(2,1)}, u32[]{:S(2)}, u32[]{:S(2)}) %collective-permute-start) | collective-permute-done | bytes 884768 | tf_op jit(solution)/shard_map/ppermute | solution.py:23
  161.0 39.1 %collective-permute-done.1 = bf16[2,1152,3,128]{3,1,2,0:T(8,128)(2,1)} collective-permute-done((bf16[2,1152,3,128]{3,1,2,0:T(8,128)(2,1)}, bf16[2,1152,3,128]{3,1,2,0:T(8,128)(2,1)}, u32[]{:S(2)}, u32[]{:S(2)}) %collective-permute-start.1) | collective-permute-done | bytes 1769504 | tf_op jit(solution)/shard_map/ppermute | solution.py:23
  200.1 5.3 %maximum_select_fusion.1 = bf16[2,2304,3,128]{3,1,2,0:T(8,128)(2,1)} fusion(bf16[2,1152,3,128]{3,1,2,0:T(8,128)(2,1)} %collective-permute-done.1, bf16[2,1152,3,128]{3,1,2,0:T(8,128)(2,1)} %maximum_select_fusion.2, pred[]{:T(512)S(6)} %eq.19), kind=kLoop, calls=%fused_computation.39 | loop fusion | flops 15925248 | bytes 7077889 | tf_op jit(solution)/shard_map/jit(_where)/select_n | solution.py:151
  211.6 71.9 %collective-permute-done.2 = bf16[2,2304,3,128]{3,1,2,0:T(8,128)(2,1)} collective-permute-done((bf16[2,2304,3,128]{3,1,2,0:T(8,128)(2,1)}, bf16[2,2304,3,128]{3,1,2,0:T(8,128)(2,1)}, u32[]{:S(2)}, u32[]{:S(2)}) %collective-permute-start.2) | collective-permute-done | bytes 3538976 | tf_op jit(solution)/shard_map/ppermute | solution.py:23
  283.5 9.3 %maximum_select_fusion = bf16[2,4608,3,128]{3,1,2,0:T(8,128)(2,1)} fusion(bf16[2,2304,3,128]{3,1,2,0:T(8,128)(2,1)} %collective-permute-done.2, bf16[2,2304,3,128]{3,1,2,0:T(8,128)(2,1)} %maximum_select_fusion.1, pred[]{:T(512)S(6)} %eq.18), kind=kLoop, calls=%fused_computation.35 | loop fusion | flops 31850496 | bytes 14155777 | tf_op jit(solution)/shard_map/jit(_where)/select_n | solution.py:151
  292.8 102.5 %while.21 = (s32[]{:T(128)}, f32[3,576]{1,0:T(4,128)S(1)}, f32[3,576]{1,0:T(4,128)S(1)}, f32[3,576,128]{2,1,0:T(8,128)}, s32[]{:T(128)}, /*index=5*/bf16[2,4608,...) while((s32[]{:T(128)}, f32[3,576]{1,0:T(4,128)S(1)}, ...), condition=%wide.region_7.8_spmd.clone.clone, body=%wide.region_4.7_spmd.clone.clone.sunk | while | flops 521231616 | bytes 15596003 | solution.py:95
  293.5 3.9 bitcast_reduce_fusion.2
  300.7 4.7 fusion.72
  306.1 3.9 bitcast_reduce_fusion.2
  313.3 5.0 fusion.72
  318.9 3.9 bitcast_reduce_fusion.2
  326.1 5.0 fusion.72
  331.7 3.9 bitcast_reduce_fusion.2
  339.0 5.0 fusion.72
  344.6 3.9 bitcast_reduce_fusion.2
  351.8 5.0 fusion.72
  357.4 3.9 bitcast_reduce_fusion.2
  364.7 5.0 fusion.72
  370.3 3.9 bitcast_reduce_fusion.2
  377.5 5.0 fusion.72
  383.1 3.9 bitcast_reduce_fusion.2
  390.3 5.0 fusion.72
  397.1 3.8 convolution_convert_fusion
  403.4 79.3 %reduce-scatter.2.cloned.1.call-done = bf16[576,768]{1,0:T(8,128)(2,1)} async-done(((bf16[576,3072]{1,0:T(8,128)(2,1)}), bf16[576,768]{1,0:T(8,128)(2,1)}) %reduce-scatter.2.cloned.1.call-update) | async-done | bytes 884752 | tf_op jit(solution)/shard_map/reduce_scatter | solution.py:162
  485.4 10.7 %all-reduce = (f32[512]{0:T(512)S(1)}, f32[512]{0:T(512)S(1)}) all-reduce(f32[512]{0:T(512)S(1)} %get-tuple-element.267, f32[512]{0:T(512)S(1)} %get-tuple-element.266), channel_id=1, replica_groups=mesh['pair'=2,'seq'=32,'tp'=4] {'tp'}, use_global_device_ids=true, to_apply=%region_12.13 | all-reduce | flops 1024 | bytes 8192 | tf_op jit(solution)/shard_map/psum | solution.py:174
  498.5 13.9 %all-gather = bf16[2048,64]{0,1:T(8,128)(2,1)S(1)} all-gather(bf16[512,64]{0,1:T(8,128)(2,1)S(1)} %fusion.38), channel_id=2, replica_groups=mesh['pair'=2,'seq'=32,'tp'=4] {'tp'}, dimensions={0}, use_global_device_ids=true | all-gather | bytes 327680 | tf_op jit(solution)/shard_map/all_gather | solution.py:181
  (117 shorter events, 79.5 us)
Async XLA Ops:
  7.2 389.9 %copy-start = (bf16[384,3072]{1,0:T(8,128)(2,1)S(1)}, bf16[384,3072]{1,0:T(8,128)(2,1)}, u32[]{:S(2)}) copy-start(bf16[384,3072]{1,0:T(8,128)(2,1)} %param.23) | copy-start | bytes 7077892
  7.2 78.7 %all-gather.3.cloned.1.call-start = ((), (), s32[]{:S(2)}) async-start(), calls=%async_computation.1 | async-start | bytes 4423680 | tf_op jit(solution)/shard_map/all_gather | solution.py:119
  7.9 474.8 %reduce-scatter.2.cloned.1.call-start = ((), (), s32[]{:S(2)}) async-start(), calls=%async_computation.2 | async-start | bytes 4423680 | tf_op jit(solution)/shard_map/reduce_scatter | solution.py:162
  8.0 10.3 %copy-start.8 = (f32[128]{0:T(128)S(1)}, f32[128]{0:T(128)}, u32[]{:S(2)}) copy-start(f32[128]{0:T(128)} %param.22) | copy-start | bytes 1540
  8.0 10.4 %copy-start.9 = (f32[128]{0:T(128)S(1)}, f32[128]{0:T(128)}, u32[]{:S(2)}) copy-start(f32[128]{0:T(128)} %param.21) | copy-start | bytes 1540
  8.0 10.6 %copy-start.7 = (s32[3,576]{1,0:T(4,128)S(1)}, s32[3,576]{1,0:T(4,128)}, u32[]{:S(2)}) copy-start(s32[3,576]{1,0:T(4,128)} %param.15) | copy-start | bytes 20740
  85.9 3.3 copy-start.1
  122.5 34.9 %collective-permute-start = (bf16[2,576,3,128]{3,1,2,0:T(8,128)(2,1)}, bf16[2,576,3,128]{3,1,2,0:T(8,128)(2,1)}, u32[]{:S(2)}, u32[]{:S(2)}) collective-permute-start(bf16[2,576,3,128]{3,1,2,0:T(8,128)(2,1)} %pad_maximum_fusion), channel_id=1, source_target_pairs={{0,4},{4,0},{8,12},{12,8},{16,20},{20,16},{24,28},{28,24},{32,36},... | collective-permute-start | bytes 2654216 | tf_op jit(solution)/shard_map/ppermute | solution.py:23
  160.4 39.7 %collective-permute-start.1 = (bf16[2,1152,3,128]{3,1,2,0:T(8,128)(2,1)}, bf16[2,1152,3,128]{3,1,2,0:T(8,128)(2,1)}, u32[]{:S(2)}, u32[]{:S(2)}) collective-permute-start(bf16[2,1152,3,128]{3,1,2,0:T(8,128)(2,1)} %maximum_select_fusion.2), channel_id=1, source_target_pairs={{0,8},{8,0},{4,12},{12,4},{16,24},{24,16},{20,28},{28,20},{32,40},... | collective-permute-start | bytes 5308424 | tf_op jit(solution)/shard_map/ppermute | solution.py:23
  161.0 46.4 %copy-start.11 = (s32[4]{0:T(128)S(1)}, s32[4]{0:T(128)}, u32[]{:S(2)}) copy-start(s32[4]{0:T(128)} %param.16) | copy-start | bytes 52
  161.0 47.0 %copy-start.4 = (bf16[576,3,64,1]{0,3,2,1:T(2,128)(2,1)S(1)}, bf16[576,3,64,1]{0,3,2,1:T(2,128)(2,1)}, u32[]{:S(2)}) copy-start(bf16[576,3,64,1]{0,3,2,1:T(2,128)(2,1)} %get-tuple-element.295) | copy-start | bytes 663556
  161.0 47.0 %copy-start.5 = (bf16[576,3,64,1]{0,3,2,1:T(2,128)(2,1)S(1)}, bf16[576,3,64,1]{0,3,2,1:T(2,128)(2,1)}, u32[]{:S(2)}) copy-start(bf16[576,3,64,1]{0,3,2,1:T(2,128)(2,1)} %get-tuple-element.296) | copy-start | bytes 663556
  205.4 78.2 %collective-permute-start.2 = (bf16[2,2304,3,128]{3,1,2,0:T(8,128)(2,1)}, bf16[2,2304,3,128]{3,1,2,0:T(8,128)(2,1)}, u32[]{:S(2)}, u32[]{:S(2)}) collective-permute-start(bf16[2,2304,3,128]{3,1,2,0:T(8,128)(2,1)} %maximum_select_fusion.1), channel_id=1, source_target_pairs={{0,16},{16,0},{4,20},{20,4},{8,24},{24,8},{12,28},{28,12},{32,48},... | collective-permute-start | bytes 10616840 | tf_op jit(solution)/shard_map/ppermute | solution.py:23
  400.8 81.8 %copy-start.2 = (bf16[576,768]{1,0:T(8,128)(2,1)S(1)}, bf16[576,768]{1,0:T(8,128)(2,1)}, u32[]{:S(2)}) copy-start(bf16[576,768]{1,0:T(8,128)(2,1)} %param.14) | copy-start | bytes 2654212
  400.8 95.3 %copy-start.10 = (bf16[768,64]{0,1:T(8,128)(2,1)S(1)}, bf16[768,64]{0,1:T(8,128)(2,1)}, u32[]{:S(2)}) copy-start(bf16[768,64]{0,1:T(8,128)(2,1)} %param.24) | copy-start | bytes 294916
  403.4 113.5 %copy-start.6 = (f32[256,64]{0,1:T(8,128)S(1)}, f32[256,64]{0,1:T(8,128)}, u32[]{:S(2)}) copy-start(f32[256,64]{0,1:T(8,128)} %param.25) | copy-start | bytes 196612
  484.1 0.9 copy-start.3
  512.9 4.0 collective-permute-start.3
Sparse Core Ops, SparseCore 0:
  9.8 76.0 all-gather.2
  401.0 81.6 reduce-scatter.1
